TPU v7x, 256 devices: a whole 4x4x8 slice. The times are simulated.
256 devices in a mesh: dp: 4 (over y), head: 4 (over x), seq: 16 (over z, core).
Axes of the slice: x: 4, y: 4, z: 8, core: 2. Of those that a mesh axis runs over, the one named last changes fastest.
Arguments:
- q_dense: bfloat16 [32768, 8, 128], P(('dp', 'seq'), 'head'), parts along dimension 0, may hold values from -108 to 108
- k_dense: bfloat16 [32768, 8, 128], P(('dp', 'seq'), 'head'), parts along dimension 0, may hold values from -4 to 4
- v_dense: bfloat16 [32768, 8, 128], P(('dp', 'seq'), 'head'), parts along dimension 0, may hold values from -4 to 4
- q_expert: bfloat16 [32768, 12, 128], P(('dp', 'seq'), 'head'), parts along dimension 0, may hold values from -108 to 108
- k_expert: bfloat16 [32768, 12, 128], P(('dp', 'seq'), 'head'), parts along dimension 0, may hold values from -4 to 4
- v_expert: bfloat16 [32768, 12, 128], P(('dp', 'seq'), 'head'), parts along dimension 0, may hold values from -4 to 4
- gate_logit: bfloat16 [12, 32768], P('head', ('dp', 'seq')), parts along dimension 1, may hold values from -8 to 8
- selection: int32 [12, 2048], P('head', 'dp'), parts along dimension 1, may hold values from 0 to 8191, as said below
Outputs:
- dense_out: bfloat16 [32768, 8, 128], P(('dp', 'seq'), 'head'), parts along dimension 0
- expert_out: bfloat16 [32768, 12, 128], P(('dp', 'seq'), 'head'), parts along dimension 0
There are 4 independent parts, one for each index of `dp`. A program takes and returns all parts, laid end to end along the dimension named above; each array names one. Nothing has to cross between parts.
Inputs may be any that keep to these rules, and one draw needn't show every extreme that they name: `selection`: each row lists 512 distinct token positions in increasing order; every row holds the first and the last token.
All inputs are finite; a program needn't handle non-finite values.
Results may differ from a plain program's by a relative error of at most 0.0055.
Values may be sent and summed in bfloat16 or wider, within the bound.
No kernel may reach another device: no remote copies, remote signals or barrier semaphores. Data moves between devices by JAX's collectives and lax.ppermute only.
A program may use at most 64 MiB of HBM per device.

v0:
```python
import math
import jax
import jax.numpy as jnp
from jax import lax
from jax.sharding import PartitionSpec as P

NEGATIVE = -1e30


def plain_rows(rows, tok_rows, count):
    return rows


def online_update(state, queries, query_pos, keys, values, key_pos, scale):
    leading, total, summed = state
    scores = jnp.einsum("qhd,khd->qhk", queries, keys, preferred_element_type=jnp.float32) * scale
    visible = key_pos[None, None, :] <= query_pos[:, None, None]
    scores = jnp.where(visible, scores, NEGATIVE)
    new_leading = jnp.maximum(leading, jnp.max(scores, axis=2))
    shrink = jnp.exp(leading - new_leading)
    weights = jnp.where(visible, jnp.exp(scores - new_leading[:, :, None]), 0.0)
    total = total * shrink + jnp.sum(weights, axis=2)
    moved = jnp.einsum(
        "qhk,khd->qhd", weights.astype(jnp.bfloat16), values, preferred_element_type=jnp.float32
    )
    return (new_leading, total, summed * shrink[:, :, None] + moved)


def dense_heads(queries, keys, values, position_map):
    tok_rows, heads, width = queries.shape
    count = lax.axis_size("seq")
    half_rows = tok_rows // 2
    own_rows = lax.axis_index("seq") * tok_rows + jnp.arange(tok_rows, dtype=jnp.int32)
    query_pos = position_map(own_rows, tok_rows, count).reshape(2, half_rows)
    groups = queries.reshape(2, half_rows, heads, width)
    scale = 1.0 / math.sqrt(width)
    blank = (
        jnp.full((half_rows, heads), NEGATIVE, jnp.float32),
        jnp.zeros((half_rows, heads), jnp.float32),
        jnp.zeros((half_rows, heads, width), jnp.float32),
    )
    key_rows = lax.all_gather(keys, "seq", axis=0, tiled=True)
    value_rows = lax.all_gather(values, "seq", axis=0, tiled=True)
    length = key_rows.shape[0]
    block = math.gcd(length, 512)
    count_blocks = length // block
    key_pos = position_map(jnp.arange(length, dtype=jnp.int32), tok_rows, count).reshape(
        count_blocks, block
    )
    key_blocks = key_rows.reshape(count_blocks, block, heads, width)
    value_blocks = value_rows.reshape(count_blocks, block, heads, width)

    def advance(state, item):
        key_block, value_block, block_pos = item
        result = []
        for group in range(2):
            seen = jnp.min(block_pos) <= jnp.max(query_pos[group])
            result.append(
                lax.cond(
                    seen,
                    lambda inner, member=group: online_update(
                        inner,
                        groups[member],
                        query_pos[member],
                        key_block,
                        value_block,
                        block_pos,
                        scale,
                    ),
                    lambda inner: inner,
                    state[group],
                )
            )
        return (tuple(result), None)

    final_state, unused = lax.scan(advance, (blank, blank), (key_blocks, value_blocks, key_pos))
    outputs = [
        (summed / total[:, :, None]).astype(jnp.bfloat16) for leading, total, summed in final_state
    ]
    return jnp.concatenate(outputs, axis=0)


def attend_ranked(query_rows, query_ranks, keys, values, gate_rows):
    heads, rows, width = query_rows.shape
    block = math.gcd(rows, 512)
    scale = 1.0 / math.sqrt(width)
    key_ranks = jnp.arange(keys.shape[1], dtype=jnp.int32)

    def one_block(index):
        scores = (
            jnp.einsum("erd,ekd->erk", query_rows, keys, preferred_element_type=jnp.float32) * scale
        )
        visible = key_ranks[None, None, :] <= query_ranks[:, :, None]
        scores = jnp.where(visible, scores, NEGATIVE)
        leading = jnp.max(scores, axis=2, keepdims=True)
        weights = jnp.where(visible, jnp.exp(scores - leading), 0.0)
        total = jnp.sum(weights, axis=2, keepdims=True)
        mixed = (
            jnp.einsum(
                "erk,ekd->erd",
                weights.astype(jnp.bfloat16),
                values,
                preferred_element_type=jnp.float32,
            )
            / total
        )
        return (mixed * jax.nn.sigmoid(gate_rows.astype(jnp.float32))[:, :, None]).astype(
            jnp.bfloat16
        )

    blocks = lax.map(one_block, jnp.arange(rows // block, dtype=jnp.int32))
    return jnp.moveaxis(blocks, 0, 1).reshape(heads, rows, width)


def sparse_heads(queries, keys, values, gate_logit, selection):
    tok_rows, heads, width = queries.shape
    chosen = selection.shape[1]
    start = lax.axis_index("seq") * tok_rows
    positions = start + jnp.arange(tok_rows, dtype=jnp.int32)
    matches = selection[:, :, None] == positions[None, None, :]
    one_hot = matches.astype(jnp.bfloat16)

    def pick(source):
        return jnp.einsum(
            "ent,ted->end", one_hot, source, preferred_element_type=jnp.float32
        ).astype(jnp.bfloat16)

    gate_rows = jnp.einsum("ent,et->en", one_hot, gate_logit, preferred_element_type=jnp.float32)
    gathered = (
        lax.psum(pick(queries), "seq").astype(jnp.float32),
        lax.psum(pick(keys), "seq").astype(jnp.float32),
        lax.psum(pick(values), "seq").astype(jnp.float32),
        lax.psum(gate_rows.astype(jnp.bfloat16), "seq").astype(jnp.float32),
    )
    picked_q, picked_k, picked_v, picked_gate = [member.astype(jnp.bfloat16) for member in gathered]
    all_ranks = jnp.broadcast_to(jnp.arange(chosen, dtype=jnp.int32)[None, :], (heads, chosen))
    results = attend_ranked(picked_q, all_ranks, picked_k, picked_v, picked_gate)
    return jnp.einsum("ent,end->ted", one_hot, results, preferred_element_type=jnp.float32).astype(
        jnp.bfloat16
    )


def local(q_dense, k_dense, v_dense, q_expert, k_expert, v_expert, gate_logit, selection):
    dense_out = dense_heads(q_dense, k_dense, v_dense, plain_rows)
    expert_out = sparse_heads(q_expert, k_expert, v_expert, gate_logit, selection)
    return (dense_out, expert_out)


def solution(mesh):
    placed = (
        P(("dp", "seq"), "head", None),
        P(("dp", "seq"), "head", None),
        P(("dp", "seq"), "head", None),
        P(("dp", "seq"), "head", None),
        P(("dp", "seq"), "head", None),
        P(("dp", "seq"), "head", None),
        P("head", ("dp", "seq")),
        P("head", "dp"),
    )
    return jax.shard_map(
        local,
        mesh=mesh,
        in_specs=placed,
        out_specs=(P(("dp", "seq"), "head", None), P(("dp", "seq"), "head", None)),
        check_vma=False,
    )
```

profile of v0, /device:TPU:225, one launch (start us, length us, event | category | flops | bytes accessed | tf_op | source)
XLA Modules:
  0.0 332.1 jit_solution(16076033150022781153)
XLA Ops:
  8.2 2.1 fusion.67
  10.3 2.5 fusion.61
  12.7 1.4 fusion.64
  16.6 23.1 %psum.31 = bf16[3,512]{1,0:T(4,128)(2,1)S(1)} all-reduce(bf16[3,512]{1,0:T(4,128)(2,1)S(1)} %bitcast.68), channel_id=1, replica_groups=mesh['dp'=4,'head'=4,'seq'=16] {'seq'}, use_global_device_ids=true, to_apply=%region_18.19 | all-reduce | flops 1536 | bytes 6144 | tf_op jit(solution)/shard_map/psum | solution.py:133
  40.3 87.0 %all-reduce.3.cloned.1.call-done = (bf16[3,512,128]{2,1,0:T(8,128)(2,1)}, bf16[3,512,128]{2,1,0:T(8,128)(2,1)}, bf16[3,512,128]{2,1,0:T(8,128)(2,1)}) async-done(((bf16[3,512,128]{2,1,0:T(8,128)(2,1)}, bf16[3,512,128]{2,1,0:T(8,128)(2,1)}, bf16[3,512,128]{2,1,0:T(8,128)(2,1)}), (bf16[3,512,128]{2,1,0:T(8,128)(2,1)}, bf16[3,512,128]{2,1,0:T(8,128)(2,1)}, ...) | async-done | bytes 1179664 | tf_op jit(solution)/shard_map/psum | solution.py:132
  127.3 2.1 fusion.90
  129.5 1.6 fusion.73
  132.0 39.2 %all-gather.3.cloned.1.call-done = bf16[8192,2,128]{2,0,1:T(8,128)(2,1)} async-done(((bf16[512,2,128]{2,0,1:T(8,128)(2,1)}), bf16[8192,2,128]{2,0,1:T(8,128)(2,1)}) %all-gather.3.cloned.1.call-update) | async-done | bytes 4194320 | tf_op jit(solution)/shard_map/all_gather | solution.py:42
  171.2 42.6 %all-gather.5.cloned.1.call-done = bf16[8192,2,128]{2,0,1:T(8,128)(2,1)} async-done(((bf16[512,2,128]{2,0,1:T(8,128)(2,1)}), bf16[8192,2,128]{2,0,1:T(8,128)(2,1)}) %all-gather.5.cloned.1.call-update) | async-done | bytes 4194320 | tf_op jit(solution)/shard_map/all_gather | solution.py:43
  213.9 109.1 %while.26 = (s32[]{:T(128)}, f32[256,2]{0,1:T(2,128)S(1)}, f32[256,2]{0,1:T(2,128)S(1)}, f32[256,2,128]{2,0,1:T(8,128)S(1)}, f32[256,2]{0,1:T(2,128)S(1)}, /*ind...) while((s32[]{:T(128)}, f32[256,2]{0,1:T(2,128)S(1)}, ...), condition=%wide.region_12.13_spmd.clone, body=%wide.region_2.12_spmd.clone.sunk | while | flops 273682432 | bytes 10830257 | solution.py:76
  215.9 1.1 dynamic-slice_bitcast_fusion.3
  217.0 1.3 conditional.6
  219.4 1.3 conditional.7
  222.7 1.1 dynamic-slice_bitcast_fusion.3
  223.8 1.3 conditional.6
  226.3 1.3 conditional.7
  229.5 1.1 dynamic-slice_bitcast_fusion.3
  230.6 1.3 conditional.6
  233.1 1.3 conditional.7
  236.3 1.1 dynamic-slice_bitcast_fusion.3
  237.4 1.3 conditional.6
  239.9 1.3 conditional.7
  244.2 1.3 conditional.6
  246.7 1.3 conditional.7
  250.0 1.1 dynamic-slice_bitcast_fusion.3
  251.0 1.3 conditional.6
  253.5 1.3 conditional.7
  257.9 1.3 conditional.6
  260.3 1.3 conditional.7
  264.7 1.3 conditional.6
  267.2 1.3 conditional.7
  271.5 1.3 conditional.6
  274.0 1.3 conditional.7
  278.3 1.3 conditional.6
  280.8 1.3 conditional.7
  285.1 1.3 conditional.6
  287.6 1.3 conditional.7
  291.9 1.3 conditional.6
  294.4 1.3 conditional.7
  298.8 1.3 conditional.6
  301.2 1.3 conditional.7
  305.6 1.3 conditional.6
  308.1 1.3 conditional.7
  312.4 1.3 conditional.6
  314.9 1.3 conditional.7
  319.2 1.3 conditional.6
  321.7 1.3 conditional.7
  323.3 1.2 fusion.82
  (341 shorter events, 67.6 us)
Async XLA Ops:
  7.2 1.0 copy-start
  7.2 5.6 %copy-start.6 = (s32[3,512]{1,0:T(4,128)S(1)}, s32[3,512]{1,0:T(4,128)}, u32[]{:S(2)}) copy-start(s32[3,512]{1,0:T(4,128)} %param.21) | copy-start | bytes 18436
  7.2 5.5 %copy-start.4 = (bf16[512,3,128]{2,0,1:T(8,128)(2,1)S(1)}, bf16[512,3,128]{2,0,1:T(8,128)(2,1)}, u32[]{:S(2)}) copy-start(bf16[512,3,128]{2,0,1:T(8,128)(2,1)} %param.18) | copy-start | bytes 1179652
  7.2 120.1 %all-reduce.3.cloned.1.call-start = ((), (), s32[]{:S(2)}) async-start(), calls=%async_computation.2 | async-start | bytes 2359296 | tf_op jit(solution)/shard_map/psum | solution.py:132
  10.3 4.0 %copy-start.1 = (bf16[512,2,128]{2,1,0:T(2,128)(2,1)S(1)}, bf16[512,2,128]{2,1,0:T(2,128)(2,1)}, u32[]{:S(2)}) copy-start(bf16[512,2,128]{2,1,0:T(2,128)(2,1)} %param.15) | copy-start | bytes 786436
  10.3 4.8 %copy-start.2 = (bf16[512,2,128]{2,1,0:T(2,128)(2,1)S(1)}, bf16[512,2,128]{2,1,0:T(2,128)(2,1)}, u32[]{:S(2)}) copy-start(bf16[512,2,128]{2,1,0:T(2,128)(2,1)} %param.16) | copy-start | bytes 786436
  10.3 5.6 %copy-start.3 = (bf16[512,2,128]{2,1,0:T(2,128)(2,1)S(1)}, bf16[512,2,128]{2,1,0:T(2,128)(2,1)}, u32[]{:S(2)}) copy-start(bf16[512,2,128]{2,1,0:T(2,128)(2,1)} %param.14) | copy-start | bytes 786436
  12.7 3.2 copy-start.7
  14.2 157.1 %all-gather.3.cloned.1.call-start = ((), (), s32[]{:S(2)}) async-start(), calls=%async_computation | async-start | bytes 4456448 | tf_op jit(solution)/shard_map/all_gather | solution.py:42
  15.0 198.9 %all-gather.5.cloned.1.call-start = ((), (), s32[]{:S(2)}) async-start(), calls=%async_computation.1 | async-start | bytes 4456448 | tf_op jit(solution)/shard_map/all_gather | solution.py:43
  127.3 2.1 copy-start.5
Sparse Core Ops, SparseCore 0:
  14.3 113.0 all-reduce.2
  129.8 41.4 all-gather.2
  173.1 40.6 all-gather.4
where the time goes:
time: 333 us; the launch traced here: 332 us
  waiting for transfers between devices  169 us (51%)
  loops' own time  42.3 us (13%)
  matrix products  36.9 us (11%)
  other arithmetic  25.7 us (8%)
  blocking collectives  23.1 us (7%)
  local copies, waits for them, and re-layouts  21.1 us (6%)
  between operations  13.9 us (4%)
    psum x1, waiting for transfers between devices, sparse_heads(): lax.psum(pick(values), 'seq').astype(jnp.float32)  87 us
    all_gather x1, waiting for transfers between devices, dense_heads(): value_rows = lax.all_gather(values, 'seq', axis=0, tiled=True)  42.6 us
    another operation x1, loops' own time, dense_heads(): lax.scan(advance, (blank, blank), (key_blocks, value_blocks, key_pos))  40.4 us
    all_gather x1, waiting for transfers between devices, dense_heads(): key_rows = lax.all_gather(keys, 'seq', axis=0, tiled=True)  39.2 us
    psum x1, blocking collectives, sparse_heads(): lax.psum(gate_rows.astype(jnp.bfloat16), 'seq').astype(jnp.float32)  23.1 us
    squeeze x16, local copies, waits for them, and re-layouts, dense_heads(): lax.scan(advance, (blank, blank), (key_blocks, value_blocks, key_pos))  17.2 us
    dot_general x32, matrix products, online_update(): jnp.einsum('qhk,khd->qhd', weights.astype(jnp.bfloat16), values, preferre...  16.5 us
    reduce_min x16, other arithmetic, advance(): seen = jnp.min(block_pos) <= jnp.max(query_pos[group])  10.3 us
  transfers between devices with their start and end apart: 3, of which 3 were waited for; matrix products, arithmetic and copies ran while one was open for 2% of the time, Pallas kernels for 0%

commit v1 on v0

--- a/solution.py
+++ b/solution.py
@@ -5,6 +5,27 @@
 from jax.sharding import PartitionSpec as P
 
 NEGATIVE = -1e30
+
+
+def collect(x, axis, dim):
+    length, index, rows = (lax.axis_size(axis), lax.axis_index(axis), x.shape[dim])
+    upward = [(i, (i + 1) % length) for i in range(length)]
+    left = [(i, (i - 1) % length) for i in range(length)]
+    out = jnp.zeros((*x.shape[:dim], length * rows, *x.shape[dim + 1 :]), x.dtype)
+    out = lax.dynamic_update_slice_in_dim(out, x, index * rows, axis=dim)
+    from_left = from_right = x
+    middle = length // 2
+    for step in range(1, middle + 1):
+        from_left = lax.ppermute(from_left, axis, upward)
+        out = lax.dynamic_update_slice_in_dim(
+            out, from_left, (index - step) % length * rows, axis=dim
+        )
+        if step < length - middle:
+            from_right = lax.ppermute(from_right, axis, left)
+            out = lax.dynamic_update_slice_in_dim(
+                out, from_right, (index + step) % length * rows, axis=dim
+            )
+    return out
 
 
 def plain_rows(rows, tok_rows, count):
@@ -39,7 +60,7 @@
         jnp.zeros((half_rows, heads), jnp.float32),
         jnp.zeros((half_rows, heads, width), jnp.float32),
     )
-    key_rows = lax.all_gather(keys, "seq", axis=0, tiled=True)
+    key_rows = collect(keys, "seq", 0)
     value_rows = lax.all_gather(values, "seq", axis=0, tiled=True)
     length = key_rows.shape[0]
     block = math.gcd(length, 512)

time: 333 us -> 296 us (0.89)
  waiting for transfers between devices: 169 us -> 88.1 us
  starting transfers between devices: 0.12 us -> 25.1 us
  local copies, waits for them, and re-layouts: 21.1 us -> 34.4 us
    all_gather x1, waiting for transfers between devices: 42.6 us -> 0.57 us  [dense_heads(): value_rows = lax.all_gather(values, 'seq', axis=0, tiled=True)]
    all_gather x1 -> x0, waiting for transfers between devices: 39.2 us -> none  [dense_heads(): key_rows = lax.all_gather(keys, 'seq', axis=0, tiled=True)]
    ppermute x0 -> x15, starting transfers between devices: none -> 25 us  [the longest x8 24.3 us: collect(): from_left = lax.ppermute(from_left, axis, upward)]
    ppermute x0 -> x15, waiting for transfers between devices: none -> 21.4 us  [the longest x7 13.3 us: collect(): from_right = lax.ppermute(from_right, axis, left)]
    psum x1, waiting for transfers between devices: 87 us -> 66.1 us  [sparse_heads(): lax.psum(pick(values), 'seq').astype(jnp.float32)]
    dynamic_update_slice x0 -> x15, local copies, waits for them, and re-layouts: none -> 10.8 us  [the longest x8 5.77 us: collect(): lax.dynamic_update_slice_in_dim(out, from_left, (index - step) % length *...]
  transfers between devices with their start and end apart: 3 -> 17, of which waited for: 3 -> 10; matrix products, arithmetic and copies ran while one was open for 2% -> 8% of each run, Pallas kernels for 0% -> 0%
where the time goes in v1:
time: 296 us; the launch traced here: 295 us
  waiting for transfers between devices  88.1 us (30%)
  loops' own time  44 us (15%)
  matrix products  39.7 us (13%)
  local copies, waits for them, and re-layouts  34.4 us (12%)
  other arithmetic  25.9 us (9%)
  starting transfers between devices  25.1 us (8%)
  blocking collectives  23.2 us (8%)
  between operations  14.3 us (5%)
    psum x1, waiting for transfers between devices, sparse_heads(): lax.psum(pick(values), 'seq').astype(jnp.float32)  66.1 us
    another operation x1, loops' own time, dense_heads(): lax.scan(advance, (blank, blank), (key_blocks, value_blocks, key_pos))  42.1 us
    ppermute x8, starting transfers between devices, collect(): from_left = lax.ppermute(from_left, axis, upward)  24.3 us
    psum x1, blocking collectives, sparse_heads(): lax.psum(gate_rows.astype(jnp.bfloat16), 'seq').astype(jnp.float32)  23.2 us
    squeeze x16, local copies, waits for them, and re-layouts, dense_heads(): lax.scan(advance, (blank, blank), (key_blocks, value_blocks, key_pos))  17.2 us
    dot_general x32, matrix products, online_update(): jnp.einsum('qhk,khd->qhd', weights.astype(jnp.bfloat16), values, preferre...  16.8 us
    ppermute x7, waiting for transfers between devices, collect(): from_right = lax.ppermute(from_right, axis, left)  13.3 us
    reduce_min x16, other arithmetic, advance(): seen = jnp.min(block_pos) <= jnp.max(query_pos[group])  10.3 us
  transfers between devices with their start and end apart: 17, of which 10 were waited for; matrix products, arithmetic and copies ran while one was open for 8% of the time, Pallas kernels for 0%

profile of v1, /device:TPU:225, one launch (start us, length us, event | category | flops | bytes accessed | tf_op | source)
XLA Modules:
  0.0 294.7 jit_solution(14679742061539861037)
XLA Ops:
  8.2 2.1 fusion.67
  10.3 2.4 fusion.61
  12.7 1.4 fusion.64
  15.0 2.5 broadcast_in_dim.84
  19.6 23.2 %psum.31 = bf16[3,512]{1,0:T(4,128)(2,1)S(1)} all-reduce(bf16[3,512]{1,0:T(4,128)(2,1)S(1)} %bitcast.67), channel_id=1, replica_groups=mesh['dp'=4,'head'=4,'seq'=16] {'seq'}, use_global_device_ids=true, to_apply=%region_18.19 | all-reduce | flops 1536 | bytes 6144 | tf_op jit(solution)/shard_map/psum | solution.py:154
  42.9 3.5 %collective-permute-start.2 = (bf16[512,2,128]{2,0,1:T(8,128)(2,1)S(1)}, bf16[512,2,128]{2,0,1:T(8,128)(2,1)S(1)}, u32[]{:S(2)}, u32[]{:S(2)}) collective-permute-start(bf16[512,2,128]{2,0,1:T(8,128)(2,1)S(1)} %collective-permute-done), channel_id=1, source_target_pairs={{0,1},{1,2},{2,3},{3,4},{4,5},{5,6},{6,7},{7,8},{8,9},{9,10},{10,1... | collective-permute-start | bytes 786440 | tf_op jit(solution)/shard_map/ppermute | solution.py:19
  48.0 2.0 collective-permute-done.2
  50.0 3.8 %collective-permute-start.4 = (bf16[512,2,128]{2,0,1:T(8,128)(2,1)S(1)}, bf16[512,2,128]{2,0,1:T(8,128)(2,1)S(1)}, u32[]{:S(2)}, u32[]{:S(2)}) collective-permute-start(bf16[512,2,128]{2,0,1:T(8,128)(2,1)S(1)} %collective-permute-done.2), channel_id=1, source_target_pairs={{0,1},{1,2},{2,3},{3,4},{4,5},{5,6},{6,7},{7,8},{8,9},{9,10},{10,1... | collective-permute-start | bytes 786440 | tf_op jit(solution)/shard_map/ppermute | solution.py:19
  56.0 1.9 collective-permute-done.4
  57.9 3.7 %collective-permute-start.6 = (bf16[512,2,128]{2,0,1:T(8,128)(2,1)S(1)}, bf16[512,2,128]{2,0,1:T(8,128)(2,1)S(1)}, u32[]{:S(2)}, u32[]{:S(2)}) collective-permute-start(bf16[512,2,128]{2,0,1:T(8,128)(2,1)S(1)} %collective-permute-done.4), channel_id=1, source_target_pairs={{0,1},{1,2},{2,3},{3,4},{4,5},{5,6},{6,7},{7,8},{8,9},{9,10},{10,1... | collective-permute-start | bytes 786440 | tf_op jit(solution)/shard_map/ppermute | solution.py:19
  61.6 66.1 %all-reduce.3.cloned.1.call-done = (bf16[3,512,128]{2,1,0:T(8,128)(2,1)}, bf16[3,512,128]{2,1,0:T(8,128)(2,1)}, bf16[3,512,128]{2,1,0:T(8,128)(2,1)}) async-done(((bf16[3,512,128]{2,1,0:T(8,128)(2,1)}, bf16[3,512,128]{2,1,0:T(8,128)(2,1)}, bf16[3,512,128]{2,1,0:T(8,128)(2,1)}), (bf16[3,512,128]{2,1,0:T(8,128)(2,1)}, bf16[3,512,128]{2,1,0:T(8,128)(2,1)}, ...) | async-done | bytes 1179664 | tf_op jit(solution)/shard_map/psum | solution.py:153
  127.7 3.3 %fusion.91 = (f32[3,512]{1,0:T(4,128)S(1)}, bf16[3,512,512]{1,2,0:T(8,128)(2,1)}) fusion(bf16[3,512,128]{2,1,0:T(8,128)(2,1)} %get-tuple-element.319, bf16[3,512,128]{2,1,0:T(8,128)(2,1)} %get-tuple-element.320), kind=kOutput, calls=%fused_computation.114 | convolution fusion | flops 207618560 | bytes 2365440 | tf_op jit(solution)/shard_map/while/body/eval_jaxpr/sub | solution.py:117
  131.0 2.9 collective-permute-start.8
  134.0 3.0 %fusion.73 = bf16[512,3,128]{0,2,1:T(8,128)(2,1)S(1)} fusion(s32[512]{0:T(512)S(1)} %iota_add_fusion, s32[3,512]{1,0:T(4,128)S(1)} %copy-done.6, bf16[3,512,128]{2,1,0:T(8,128)(2,1)S(1)} %copy-done.5, bf16[3,512,512]{1,2,0:T(8,128)(2,1)} %get-tuple-element.336, f32[3,512]{1,0:T(4,128)S(1)} %add_divide_fusion, f32[3,512]{1,0:T(4,128)S(1)} %get-tuple-element.335), kind=kOutput, calls=%fused_computation.75 | convolution fusion | flops 404226048 | bytes 2379776 | tf_op jit(solution)/shard_map/ent,end->ted/dot_general | solution.py:159
  138.7 3.0 %collective-permute-start.10 = (bf16[512,2,128]{2,0,1:T(8,128)(2,1)S(1)}, bf16[512,2,128]{2,0,1:T(8,128)(2,1)S(1)}, u32[]{:S(2)}, u32[]{:S(2)}) collective-permute-start(bf16[512,2,128]{2,0,1:T(8,128)(2,1)S(1)} %collective-permute-done.8), channel_id=1, source_target_pairs={{0,1},{1,2},{2,3},{3,4},{4,5},{5,6},{6,7},{7,8},{8,9},{9,10},{10,1... | collective-permute-start | bytes 786440 | tf_op jit(solution)/shard_map/ppermute | solution.py:19
  143.1 4.4 %collective-permute-done.9 = bf16[512,2,128]{2,0,1:T(8,128)(2,1)S(1)} collective-permute-done((bf16[512,2,128]{2,0,1:T(8,128)(2,1)S(1)}, bf16[512,2,128]{2,0,1:T(8,128)(2,1)S(1)}, u32[]{:S(2)}, u32[]{:S(2)}) %collective-permute-start.9) | collective-permute-done | bytes 262176 | tf_op jit(solution)/shard_map/ppermute | solution.py:24
  148.3 2.1 collective-permute-done.10
  150.4 3.7 %collective-permute-start.12 = (bf16[512,2,128]{2,0,1:T(8,128)(2,1)S(1)}, bf16[512,2,128]{2,0,1:T(8,128)(2,1)S(1)}, u32[]{:S(2)}, u32[]{:S(2)}) collective-permute-start(bf16[512,2,128]{2,0,1:T(8,128)(2,1)S(1)} %collective-permute-done.10), channel_id=1, source_target_pairs={{0,1},{1,2},{2,3},{3,4},{4,5},{5,6},{6,7},{7,8},{8,9},{9,10},{10,1... | collective-permute-start | bytes 786440 | tf_op jit(solution)/shard_map/ppermute | solution.py:19
  155.5 4.4 %collective-permute-done.11 = bf16[512,2,128]{2,0,1:T(8,128)(2,1)S(1)} collective-permute-done((bf16[512,2,128]{2,0,1:T(8,128)(2,1)S(1)}, bf16[512,2,128]{2,0,1:T(8,128)(2,1)S(1)}, u32[]{:S(2)}, u32[]{:S(2)}) %collective-permute-start.11) | collective-permute-done | bytes 262176 | tf_op jit(solution)/shard_map/ppermute | solution.py:24
  160.6 2.0 collective-permute-done.12
  162.7 3.7 %collective-permute-start.14 = (bf16[512,2,128]{2,0,1:T(8,128)(2,1)S(1)}, bf16[512,2,128]{2,0,1:T(8,128)(2,1)S(1)}, u32[]{:S(2)}, u32[]{:S(2)}) collective-permute-start(bf16[512,2,128]{2,0,1:T(8,128)(2,1)S(1)} %collective-permute-done.12), channel_id=1, source_target_pairs={{0,1},{1,2},{2,3},{3,4},{4,5},{5,6},{6,7},{7,8},{8,9},{9,10},{10,1... | collective-permute-start | bytes 786440 | tf_op jit(solution)/shard_map/ppermute | solution.py:19
  167.8 4.4 %collective-permute-done.13 = bf16[512,2,128]{2,0,1:T(8,128)(2,1)S(1)} collective-permute-done((bf16[512,2,128]{2,0,1:T(8,128)(2,1)S(1)}, bf16[512,2,128]{2,0,1:T(8,128)(2,1)S(1)}, u32[]{:S(2)}, u32[]{:S(2)}) %collective-permute-start.13) | collective-permute-done | bytes 262176 | tf_op jit(solution)/shard_map/ppermute | solution.py:24
  174.3 111.0 %while.26 = (s32[]{:T(128)}, f32[256,2]{0,1:T(2,128)S(1)}, f32[256,2]{0,1:T(2,128)S(1)}, f32[256,2,128]{2,0,1:T(8,128)S(1)}, f32[256,2]{0,1:T(2,128)S(1)}, /*ind...) while((s32[]{:T(128)}, f32[256,2]{0,1:T(2,128)S(1)}, ...), condition=%wide.region_12.13_spmd.clone, body=%wide.region_2.12_spmd.clone.sunk | while | flops 273682432 | bytes 10830257 | solution.py:97
  177.4 1.3 conditional.6
  179.9 1.3 conditional.7
  184.3 1.3 conditional.6
  191.2 1.3 conditional.6
  193.8 1.3 conditional.7
  198.2 1.3 conditional.6
  200.7 1.3 conditional.7
  205.1 1.3 conditional.6
  212.1 1.3 conditional.6
  214.6 1.3 conditional.7
  219.0 1.3 conditional.6
  221.6 1.3 conditional.7
  225.9 1.3 conditional.6
  232.9 1.3 conditional.6
  235.4 1.3 conditional.7
  239.8 1.3 conditional.6
  242.4 1.3 conditional.7
  246.8 1.3 conditional.6
  253.7 1.3 conditional.6
  260.6 1.3 conditional.6
  263.2 1.3 conditional.7
  267.6 1.3 conditional.6
  274.5 1.3 conditional.6
  281.4 1.3 conditional.6
  284.0 1.3 conditional.7
  (384 shorter events, 95.8 us)
Async XLA Ops:
  7.2 1.0 copy-start
  7.2 5.5 %copy-start.6 = (s32[3,512]{1,0:T(4,128)S(1)}, s32[3,512]{1,0:T(4,128)}, u32[]{:S(2)}) copy-start(s32[3,512]{1,0:T(4,128)} %param.21) | copy-start | bytes 18436
  7.2 5.5 %copy-start.4 = (bf16[512,3,128]{2,0,1:T(8,128)(2,1)S(1)}, bf16[512,3,128]{2,0,1:T(8,128)(2,1)}, u32[]{:S(2)}) copy-start(bf16[512,3,128]{2,0,1:T(8,128)(2,1)} %param.18) | copy-start | bytes 1179652
  7.2 7.0 %copy-start.1 = (bf16[512,2,128]{2,1,0:T(2,128)(2,1)S(1)}, bf16[512,2,128]{2,1,0:T(2,128)(2,1)}, u32[]{:S(2)}) copy-start(bf16[512,2,128]{2,1,0:T(2,128)(2,1)} %param.16) | copy-start | bytes 786436
  7.2 120.4 %all-reduce.3.cloned.1.call-start = ((), (), s32[]{:S(2)}) async-start(), calls=%async_computation.1 | async-start | bytes 2359296 | tf_op jit(solution)/shard_map/psum | solution.py:153
  12.7 4.8 %copy-start.3 = (bf16[512,2,128]{2,1,0:T(2,128)(2,1)S(1)}, bf16[512,2,128]{2,1,0:T(2,128)(2,1)}, u32[]{:S(2)}) copy-start(bf16[512,2,128]{2,1,0:T(2,128)(2,1)} %param.15) | copy-start | bytes 786436
  12.7 6.3 %copy-start.7 = (bf16[3,512]{1,0:T(4,128)(2,1)S(1)}, bf16[3,512]{1,0:T(4,128)(2,1)}, u32[]{:S(2)}) copy-start(bf16[3,512]{1,0:T(4,128)(2,1)} %param.20) | copy-start | bytes 9220
  14.1 33.0 %copy-start.2 = (bf16[512,2,128]{2,1,0:T(2,128)(2,1)S(1)}, bf16[512,2,128]{2,1,0:T(2,128)(2,1)}, u32[]{:S(2)}) copy-start(bf16[512,2,128]{2,1,0:T(2,128)(2,1)} %param.14) | copy-start | bytes 786436
  14.2 160.0 %all-gather.2.cloned.1.call-start = ((), (), s32[]{:S(2)}) async-start(), calls=%async_computation | async-start | bytes 4456448 | tf_op jit(solution)/shard_map/all_gather | solution.py:64
  18.3 24.6 %collective-permute-start = (bf16[512,2,128]{2,0,1:T(8,128)(2,1)S(1)}, bf16[512,2,128]{2,0,1:T(8,128)(2,1)S(1)}, u32[]{:S(2)}, u32[]{:S(2)}) collective-permute-start(bf16[512,2,128]{2,0,1:T(8,128)(2,1)S(1)} %get-tuple-element.333), channel_id=1, source_target_pairs={{0,1},{1,2},{2,3},{3,4},{4,5},{5,6},{6,7},{7,8},{8,9},{9,10},{10,1... | collective-permute-start | bytes 786440 | tf_op jit(solution)/shard_map/ppermute | solution.py:19
  18.3 28.1 %collective-permute-start.1 = (bf16[512,2,128]{2,0,1:T(8,128)(2,1)S(1)}, bf16[512,2,128]{2,0,1:T(8,128)(2,1)S(1)}, u32[]{:S(2)}, u32[]{:S(2)}) collective-permute-start(bf16[512,2,128]{2,0,1:T(8,128)(2,1)S(1)} %get-tuple-element.333), channel_id=1, source_target_pairs={{0,15},{1,0},{2,1},{3,2},{4,3},{5,4},{6,5},{7,6},{8,7},{9,8},{10,9... | collective-permute-start | bytes 786440 | tf_op jit(solution)/shard_map/ppermute | solution.py:24
  42.9 7.1 %collective-permute-start.2 = (bf16[512,2,128]{2,0,1:T(8,128)(2,1)S(1)}, bf16[512,2,128]{2,0,1:T(8,128)(2,1)S(1)}, u32[]{:S(2)}, u32[]{:S(2)}) collective-permute-start(bf16[512,2,128]{2,0,1:T(8,128)(2,1)S(1)} %collective-permute-done), channel_id=1, source_target_pairs={{0,1},{1,2},{2,3},{3,4},{4,5},{5,6},{6,7},{7,8},{8,9},{9,10},{10,1... | collective-permute-start | bytes 786440 | tf_op jit(solution)/shard_map/ppermute | solution.py:19
  46.4 8.1 %collective-permute-start.3 = (bf16[512,2,128]{2,0,1:T(8,128)(2,1)S(1)}, bf16[512,2,128]{2,0,1:T(8,128)(2,1)S(1)}, u32[]{:S(2)}, u32[]{:S(2)}) collective-permute-start(bf16[512,2,128]{2,0,1:T(8,128)(2,1)S(1)} %collective-permute-done.1), channel_id=1, source_target_pairs={{0,15},{1,0},{2,1},{3,2},{4,3},{5,4},{6,5},{7,6},{8,7},{9,8},{10,9... | collective-permute-start | bytes 786440 | tf_op jit(solution)/shard_map/ppermute | solution.py:24
  50.0 7.9 %collective-permute-start.4 = (bf16[512,2,128]{2,0,1:T(8,128)(2,1)S(1)}, bf16[512,2,128]{2,0,1:T(8,128)(2,1)S(1)}, u32[]{:S(2)}, u32[]{:S(2)}) collective-permute-start(bf16[512,2,128]{2,0,1:T(8,128)(2,1)S(1)} %collective-permute-done.2), channel_id=1, source_target_pairs={{0,1},{1,2},{2,3},{3,4},{4,5},{5,6},{6,7},{7,8},{8,9},{9,10},{10,1... | collective-permute-start | bytes 786440 | tf_op jit(solution)/shard_map/ppermute | solution.py:19
  54.5 76.5 %collective-permute-start.5 = (bf16[512,2,128]{2,0,1:T(8,128)(2,1)S(1)}, bf16[512,2,128]{2,0,1:T(8,128)(2,1)S(1)}, u32[]{:S(2)}, u32[]{:S(2)}) collective-permute-start(bf16[512,2,128]{2,0,1:T(8,128)(2,1)S(1)} %collective-permute-done.3), channel_id=1, source_target_pairs={{0,15},{1,0},{2,1},{3,2},{4,3},{5,4},{6,5},{7,6},{8,7},{9,8},{10,9... | collective-permute-start | bytes 786440 | tf_op jit(solution)/shard_map/ppermute | solution.py:24
  57.9 73.1 %collective-permute-start.6 = (bf16[512,2,128]{2,0,1:T(8,128)(2,1)S(1)}, bf16[512,2,128]{2,0,1:T(8,128)(2,1)S(1)}, u32[]{:S(2)}, u32[]{:S(2)}) collective-permute-start(bf16[512,2,128]{2,0,1:T(8,128)(2,1)S(1)} %collective-permute-done.4), channel_id=1, source_target_pairs={{0,1},{1,2},{2,3},{3,4},{4,5},{5,6},{6,7},{7,8},{8,9},{9,10},{10,1... | collective-permute-start | bytes 786440 | tf_op jit(solution)/shard_map/ppermute | solution.py:19
  127.7 6.3 %copy-start.5 = (bf16[3,512,128]{2,1,0:T(8,128)(2,1)S(1)}, bf16[3,512,128]{2,1,0:T(8,128)(2,1)}, u32[]{:S(2)}) copy-start(bf16[3,512,128]{2,1,0:T(8,128)(2,1)} %get-tuple-element.318) | copy-start | bytes 1179652
  131.0 7.0 %collective-permute-start.7 = (bf16[512,2,128]{2,0,1:T(8,128)(2,1)S(1)}, bf16[512,2,128]{2,0,1:T(8,128)(2,1)S(1)}, u32[]{:S(2)}, u32[]{:S(2)}) collective-permute-start(bf16[512,2,128]{2,0,1:T(8,128)(2,1)S(1)} %collective-permute-done.5), channel_id=1, source_target_pairs={{0,15},{1,0},{2,1},{3,2},{4,3},{5,4},{6,5},{7,6},{8,7},{9,8},{10,9... | collective-permute-start | bytes 786440 | tf_op jit(solution)/shard_map/ppermute | solution.py:24
  131.0 7.7 %collective-permute-start.8 = (bf16[512,2,128]{2,0,1:T(8,128)(2,1)S(1)}, bf16[512,2,128]{2,0,1:T(8,128)(2,1)S(1)}, u32[]{:S(2)}, u32[]{:S(2)}) collective-permute-start(bf16[512,2,128]{2,0,1:T(8,128)(2,1)S(1)} %collective-permute-done.6), channel_id=1, source_target_pairs={{0,1},{1,2},{2,3},{3,4},{4,5},{5,6},{6,7},{7,8},{8,9},{9,10},{10,1... | collective-permute-start | bytes 786440 | tf_op jit(solution)/shard_map/ppermute | solution.py:19
  138.0 9.6 %collective-permute-start.9 = (bf16[512,2,128]{2,0,1:T(8,128)(2,1)S(1)}, bf16[512,2,128]{2,0,1:T(8,128)(2,1)S(1)}, u32[]{:S(2)}, u32[]{:S(2)}) collective-permute-start(bf16[512,2,128]{2,0,1:T(8,128)(2,1)S(1)} %collective-permute-done.7), channel_id=1, source_target_pairs={{0,15},{1,0},{2,1},{3,2},{4,3},{5,4},{6,5},{7,6},{8,7},{9,8},{10,9... | collective-permute-start | bytes 786440 | tf_op jit(solution)/shard_map/ppermute | solution.py:24
  138.7 11.7 %collective-permute-start.10 = (bf16[512,2,128]{2,0,1:T(8,128)(2,1)S(1)}, bf16[512,2,128]{2,0,1:T(8,128)(2,1)S(1)}, u32[]{:S(2)}, u32[]{:S(2)}) collective-permute-start(bf16[512,2,128]{2,0,1:T(8,128)(2,1)S(1)} %collective-permute-done.8), channel_id=1, source_target_pairs={{0,1},{1,2},{2,3},{3,4},{4,5},{5,6},{6,7},{7,8},{8,9},{9,10},{10,1... | collective-permute-start | bytes 786440 | tf_op jit(solution)/shard_map/ppermute | solution.py:19
  147.6 12.3 %collective-permute-start.11 = (bf16[512,2,128]{2,0,1:T(8,128)(2,1)S(1)}, bf16[512,2,128]{2,0,1:T(8,128)(2,1)S(1)}, u32[]{:S(2)}, u32[]{:S(2)}) collective-permute-start(bf16[512,2,128]{2,0,1:T(8,128)(2,1)S(1)} %collective-permute-done.9), channel_id=1, source_target_pairs={{0,15},{1,0},{2,1},{3,2},{4,3},{5,4},{6,5},{7,6},{8,7},{9,8},{10,9... | collective-permute-start | bytes 786440 | tf_op jit(solution)/shard_map/ppermute | solution.py:24
  150.4 12.3 %collective-permute-start.12 = (bf16[512,2,128]{2,0,1:T(8,128)(2,1)S(1)}, bf16[512,2,128]{2,0,1:T(8,128)(2,1)S(1)}, u32[]{:S(2)}, u32[]{:S(2)}) collective-permute-start(bf16[512,2,128]{2,0,1:T(8,128)(2,1)S(1)} %collective-permute-done.10), channel_id=1, source_target_pairs={{0,1},{1,2},{2,3},{3,4},{4,5},{5,6},{6,7},{7,8},{8,9},{9,10},{10,1... | collective-permute-start | bytes 786440 | tf_op jit(solution)/shard_map/ppermute | solution.py:19
  159.9 12.3 %collective-permute-start.13 = (bf16[512,2,128]{2,0,1:T(8,128)(2,1)S(1)}, bf16[512,2,128]{2,0,1:T(8,128)(2,1)S(1)}, u32[]{:S(2)}, u32[]{:S(2)}) collective-permute-start(bf16[512,2,128]{2,0,1:T(8,128)(2,1)S(1)} %collective-permute-done.11), channel_id=1, source_target_pairs={{0,15},{1,0},{2,1},{3,2},{4,3},{5,4},{6,5},{7,6},{8,7},{9,8},{10,9... | collective-permute-start | bytes 786440 | tf_op jit(solution)/shard_map/ppermute | solution.py:24
  162.7 10.2 %collective-permute-start.14 = (bf16[512,2,128]{2,0,1:T(8,128)(2,1)S(1)}, bf16[512,2,128]{2,0,1:T(8,128)(2,1)S(1)}, u32[]{:S(2)}, u32[]{:S(2)}) collective-permute-start(bf16[512,2,128]{2,0,1:T(8,128)(2,1)S(1)} %collective-permute-done.12), channel_id=1, source_target_pairs={{0,1},{1,2},{2,3},{3,4},{4,5},{5,6},{6,7},{7,8},{8,9},{9,10},{10,1... | collective-permute-start | bytes 786440 | tf_op jit(solution)/shard_map/ppermute | solution.py:19
Sparse Core Ops, SparseCore 0:
  14.3 113.3 all-reduce.2
  130.1 44.0 all-gather.1
